TPU v7x, 512 devices: a whole 4x8x8 slice. The times are simulated.
512 devices in a mesh: rep: 8 (over y_lo, core), seq: 2 (over y_hi), tp: 32 (over x, z).
Axes of the slice: x: 4, y: 8 (y_hi: 2, y_lo: 4; y = y_hi * 4 + y_lo), z: 8, core: 2. Of those that a mesh axis runs over, the one named last changes fastest.
Arguments:
- hidden: bfloat16 [3072, 8192], P('rep', ('seq', 'tp')), may hold values from -100 to 100
- gain: float32 [8192], replicated, may hold values from 0.1 to 1.9
- w_query: bfloat16 [8192, 8192], P('seq', 'tp'), may hold values from -1 to 1
- w_keyval: bfloat16 [2, 4096, 2048], P(None, 'tp'), may hold values from -1 to 1
- lengths: int32 [8, 2], replicated, may hold values from 128 to 192, as said below
- routes: int32 [8, 2], replicated, may hold values from 0 to 7, as said below
Outputs:
- attended: bfloat16 [3072, 8192], P(('rep', 'seq'), 'tp')
Inputs may be any that keep to these rules, and one draw needn't show every extreme that they name: `routes`: for each j, the responses j of the 8 rollout groups go to 8 different replicas, so each replica receives exactly 2 responses. `lengths`: the responses that one rollout group sends to one replica hold at most 192 tokens together, and in every draw some group sends exactly 192 tokens to one replica.
All inputs are finite; a program needn't handle non-finite values.
Results may differ from a plain program's by a relative error of at most 0.0076.
Values may be sent and summed in bfloat16 or wider, within the bound.
No kernel may reach another device: no remote copies, remote signals or barrier semaphores. Data moves between devices by JAX's collectives and lax.ppermute only.
A program may use at most 64 MiB of HBM per device.

v0:
```python
import math
import jax
import jax.numpy as jnp
from jax import lax
from jax.sharding import PartitionSpec as P

D = 8192
QH = 64
KVH = 8
HD = 128
RESP = 2
LMAX = 192
BUFFER = 384
ROPE_BASE = 500000.0
NORM_EPS = 1e-05
MASK_FILL = -1e30


def response_tables(lengths, routes):
    flat_len = lengths.reshape(-1)
    flat_route = routes.reshape(-1)
    response_ids = jnp.arange(flat_len.shape[0], dtype=jnp.int32)
    group_of = response_ids // RESP
    same_route = flat_route[:, None] == flat_route[None, :]
    same_group = group_of[:, None] == group_of[None, :]
    earlier = response_ids[None, :] < response_ids[:, None]
    dest_off = jnp.sum(jnp.where(same_route & earlier, flat_len[None, :], 0), axis=1)
    pair_off = jnp.sum(jnp.where(same_route & same_group & earlier, flat_len[None, :], 0), axis=1)
    src_start = jnp.sum(jnp.where(same_group & earlier, flat_len[None, :], 0), axis=1)
    return (flat_len, flat_route, group_of, dest_off, pair_off, src_start)


def locate(positions, replica, tables):
    flat_len, flat_route, group_of, dest_off, pair_off, src_start = tables
    response_ids = jnp.arange(flat_len.shape[0], dtype=jnp.int32)
    position_col = positions[:, None]
    inside = (
        (flat_route[None, :] == replica)
        & (dest_off[None, :] <= position_col)
        & (position_col < dest_off[None, :] + flat_len[None, :])
    )
    inside_int = inside.astype(jnp.int32)
    segment = jnp.sum(inside_int * (response_ids[None, :] + 1), axis=1) - 1
    seg_start = jnp.sum(inside_int * dest_off[None, :], axis=1)
    source_group = jnp.sum(inside_int * group_of[None, :], axis=1)
    pair_first = jnp.sum(inside_int * (dest_off - pair_off)[None, :], axis=1)
    source = jnp.sum(inside_int * src_start[None, :], axis=1)
    within = jnp.where(segment >= 0, positions - seg_start, 0)
    return (segment, within, source_group, pair_first, source)


def rotary(values_in, within):
    head_dim = values_in.shape[-1]
    half_dim = head_dim // 2
    freq_index = jnp.arange(half_dim, dtype=jnp.float32)
    inverse = jnp.power(ROPE_BASE, -2.0 * freq_index / head_dim)
    angles = within.astype(jnp.float32)[:, None] * inverse[None, :]
    cosine = jnp.cos(angles)[:, None, :]
    sine_part = jnp.sin(angles)[:, None, :]
    lower_half = values_in[..., :half_dim]
    upper_half = values_in[..., half_dim:]
    return jnp.concatenate(
        [
            lower_half * cosine - upper_half * sine_part,
            upper_half * cosine + lower_half * sine_part,
        ],
        axis=-1,
    )


def fill_rows(table, indices, present):
    taken = jnp.take(table, indices.reshape(-1), axis=0)
    return jnp.where(present.reshape(-1)[:, None], taken, jnp.zeros((), table.dtype))


def local(hidden, gain, w_query, w_keyval, lengths, routes):
    rep_count = lax.axis_size("rep")
    seq_count = lax.axis_size("seq")
    replica = lax.axis_index("rep")
    seq_index = lax.axis_index("seq")
    column = lax.axis_index("tp")
    feature_cols = hidden.shape[1]
    local_rows = BUFFER // seq_count
    capacity = (RESP + rep_count - 1) // rep_count * LMAX
    head_count = w_query.shape[1] // HD
    tables = response_tables(lengths, routes)
    flat_len, flat_route, group_of, dest_off, pair_off, src_start = tables
    my_len = lax.dynamic_slice_in_dim(flat_len, replica * RESP, RESP)
    my_route = lax.dynamic_slice_in_dim(flat_route, replica * RESP, RESP)
    my_pair = lax.dynamic_slice_in_dim(pair_off, replica * RESP, RESP)
    my_start = lax.dynamic_slice_in_dim(src_start, replica * RESP, RESP)
    slot_ids = jnp.arange(capacity, dtype=jnp.int32)
    targets = jnp.arange(rep_count, dtype=jnp.int32)
    block_off = jnp.broadcast_to(slot_ids[None, :], (rep_count, capacity))
    offsets = block_off[:, :, None]
    inside = (
        (my_route[None, None, :] == targets[:, None, None])
        & (my_pair[None, None, :] <= offsets)
        & (offsets < (my_pair + my_len)[None, None, :])
    )
    inside_int = inside.astype(jnp.int32)
    src_rows = jnp.sum(
        inside_int * (my_start[None, None, :] + offsets - my_pair[None, None, :]), axis=2
    )
    src_rows, present = (src_rows, jnp.any(inside, axis=2))
    outgoing = fill_rows(hidden, src_rows, present)
    incoming = lax.all_to_all(outgoing, "rep", split_axis=0, concat_axis=0, tiled=True)
    all_pos = jnp.arange(BUFFER, dtype=jnp.int32)
    segment, within, source_group, pair_first, source = locate(all_pos, replica, tables)
    gathered_idx = jnp.where(segment >= 0, source_group * capacity + all_pos - pair_first, 0)
    assembled = fill_rows(incoming, gathered_idx, segment >= 0)
    local_x = lax.all_to_all(
        assembled.reshape(BUFFER, 1, feature_cols), "seq", split_axis=0, concat_axis=1, tiled=True
    )
    query_pos = seq_index * local_rows + jnp.arange(local_rows, dtype=jnp.int32)
    query_info = locate(query_pos, replica, tables)
    query_seg = query_info[0]
    query_within = query_info[1]
    query_valid = query_seg >= 0
    gain_halves = gain.reshape(seq_count, D // seq_count)
    gain_local = lax.dynamic_slice_in_dim(gain_halves, column * feature_cols, feature_cols, 1)
    kv_head = column * head_count // (QH // KVH)
    query_weights = lax.all_gather(
        w_query.reshape(1, w_query.shape[0], w_query.shape[1]), "seq", axis=0, tiled=True
    )
    feature_piece = lax.all_gather(local_x, "tp", axis=2, tiled=True)
    scaled_piece = (feature_piece.astype(jnp.float32) * gain_halves[None]).astype(jnp.bfloat16)
    query_acc = jnp.einsum(
        "rsn,snf->rf", scaled_piece, query_weights, preferred_element_type=jnp.float32
    )
    squares = jnp.sum(jnp.square(feature_piece.astype(jnp.float32)), axis=(1, 2))
    inverse_rms = lax.rsqrt(squares / D + NORM_EPS)
    queries = rotary(
        inverse_rms[:, None, None] * query_acc.reshape(local_rows, head_count, HD), query_within
    ).astype(jnp.bfloat16)
    scaled_local = (local_x.astype(jnp.float32) * gain_local[None]).astype(jnp.bfloat16)
    kv_partial = jnp.einsum(
        "rsw,swc->rc", scaled_local, w_keyval, preferred_element_type=jnp.float32
    )
    kv_total = lax.psum(kv_partial, "tp")
    head_block = lax.dynamic_slice_in_dim(kv_total, kv_head * 2 * HD, 2 * HD, 1)
    keys = rotary(inverse_rms[:, None, None] * head_block[:, None, :HD], query_within)[:, 0].astype(
        jnp.bfloat16
    )
    values = (inverse_rms[:, None] * head_block[:, HD:]).astype(jnp.bfloat16)
    score_scale = 1.0 / math.sqrt(HD)
    running = jnp.full((local_rows, head_count), MASK_FILL, jnp.float32)
    key_part = lax.all_gather(keys, "seq", axis=0, tiled=True)
    value_part = lax.all_gather(values, "seq", axis=0, tiled=True)
    key_count = key_part.shape[0]
    key_pos = jnp.arange(key_count, dtype=jnp.int32)
    key_seg = locate(key_pos, replica, tables)[0]
    allowed = (key_seg[None, :] == query_seg[:, None]) & query_valid[:, None] & (
        key_pos[None, :] <= query_pos[:, None]
    ) | (key_pos[None, :] == query_pos[:, None])
    scores = (
        jnp.einsum("rhd,kd->rhk", queries, key_part, preferred_element_type=jnp.float32)
        * score_scale
    )
    scores = jnp.where(allowed[:, None, :], scores, MASK_FILL)
    new_max = jnp.maximum(running, jnp.max(scores, axis=2))
    prob_terms = jnp.where(allowed[:, None, :], jnp.exp(scores - new_max[:, :, None]), 0.0)
    totals = jnp.sum(prob_terms, axis=2)
    accum = jnp.einsum(
        "rhk,kd->rhd",
        prob_terms.astype(jnp.bfloat16),
        value_part,
        preferred_element_type=jnp.float32,
    )
    attended = (
        (accum / totals[:, :, None]).reshape(local_rows, head_count * HD).astype(jnp.bfloat16)
    )
    return jnp.where(query_valid[:, None], attended, jnp.zeros((), jnp.bfloat16))


def solution(mesh):
    in_specs = (P("rep", ("seq", "tp")), P(), P("seq", "tp"), P(None, "tp", None), P(), P())
    out_specs = P(("rep", "seq"), "tp")
    return jax.shard_map(local, mesh=mesh, in_specs=in_specs, out_specs=out_specs, check_vma=False)
```

profile of v0, /device:TPU:16, one launch (start us, length us, event | category | flops | bytes accessed | tf_op | source)
XLA Modules:
  0.0 440.9 jit_solution(4229495986316716021)
XLA Ops:
  6.5 0.0 copy-start
  6.5 0.8 copy.25
  7.4 0.1 broadcast_in_dim.98
  7.5 0.8 copy.24
  8.2 0.1 broadcast_in_dim_reshape.2
  8.3 0.1 dynamic_slice.18
  8.4 0.2 select_reduce_fusion.7
  8.6 0.1 dynamic-slice_add_fusion
  8.7 0.1 dynamic_slice.21
  8.8 0.1 iota_compare_fusion.7
  8.8 0.1 select_reduce_fusion.4
  8.9 0.1 reshape.451
  9.0 0.1 fusion.43
  9.1 3.5 gather_fusion
  12.7 0.0 copy-start.1
  12.7 1.3 select_select_fusion
  14.0 9.1 %all-to-all-start = ((bf16[8,192,128]{2,1,0:T(8,128)(2,1)}), bf16[8,192,128]{2,1,0:T(8,128)(2,1)S(1)}, u32[]{:S(2)}, u32[]{:S(2)}) async-start(bf16[8,192,128]{2,1,0:T(8,128)(2,1)} %select_select_fusion), calls=%async_computation | async-start | bytes 786432 | tf_op jit(solution)/shard_map/all_to_all | solution.py:107
  23.1 0.0 all-gather.6.cloned.1.call-start
  23.1 0.1 select_reduce_fusion.1
  23.3 9.1 %all-to-all-done = bf16[8,192,128]{2,1,0:T(8,128)(2,1)S(1)} async-done(((bf16[8,192,128]{2,1,0:T(8,128)(2,1)}), bf16[8,192,128]{2,1,0:T(8,128)(2,1)S(1)}, u32[]{:S(2)}, u32[]{:S(2)}) %all-to-all-start) | async-done | bytes 393248 | tf_op jit(solution)/shard_map/all_to_all | solution.py:107
  32.4 1.4 gather_fusion.1
  33.8 0.2 fusion.37
  34.0 0.5 broadcast.494
  34.5 0.7 reduce.4
  35.2 10.6 %all_to_all.27 = bf16[2,2,12288]{2,1,0:T(2,128)(2,1)S(1)} all-to-all(bf16[2,2,12288]{2,1,0:T(2,128)(2,1)S(1)} %reshape.481), channel_id=1, replica_groups=mesh['rep'=8,'seq'=2,'tp'=32] {'seq'}, dimensions={0} | all-to-all | bytes 196608 | tf_op jit(solution)/shard_map/all_to_all | solution.py:112
  45.8 0.1 reshape.482
  45.9 0.7 copy.29
  46.5 0.0 all-gather.6.cloned.1.call-update
  46.6 0.0 all-gather.8.cloned.1.call-start
  46.6 0.7 all-gather.8.cloned.1.call-update
  47.3 0.0 all-reduce.2.cloned.1.call-start
  47.4 0.0 copy-done.1
  47.5 0.1 select_reduce_fusion.3
  47.6 0.2 fusion.18
  47.8 0.0 copy-done
  47.8 2.5 convolution_bitcast_fusion
  50.2 0.0 all-reduce.2.cloned.1.call-update
  50.3 0.4 multiply_cosine_fusion.1
  50.7 82.6 %all-gather.6.cloned.1.call-done = bf16[192,2,1,4096]{3,0,1,2:T(8,128)(2,1)} async-done(((bf16[192,2,1,128]{3,0,1,2:T(8,128)(2,1)}), bf16[192,2,1,4096]{3,0,1,2:T(8,128)(2,1)}) %all-gather.6.cloned.1.call-update) | async-done | bytes 3145744 | tf_op jit(solution)/shard_map/all_gather | solution.py:126
  133.3 2.6 fusion
  135.9 111.5 %all-gather.8.cloned.1.call-done = bf16[8192,256]{1,0:T(8,128)(2,1)} async-done(((bf16[4096,256]{1,0:T(8,128)(2,1)}), bf16[8192,256]{1,0:T(8,128)(2,1)}) %all-gather.8.cloned.1.call-update) | async-done | bytes 4194320 | tf_op jit(solution)/shard_map/all_gather | solution.py:123
  247.4 4.1 fusion.7
  251.6 0.1 bitcast_multiply_fusion
  251.7 161.3 %all-reduce.2.cloned.1.call-done = f32[192,2048]{1,0:T(8,128)} async-done(((f32[192,2048]{1,0:T(8,128)}), f32[192,2048]{1,0:T(8,128)}) %all-reduce.2.cloned.1.call-update) | async-done | bytes 1572880 | tf_op jit(solution)/shard_map/psum | solution.py:140
  412.9 1.0 fusion.30
  413.9 0.5 fusion.26
  414.4 0.1 pad_maximum_fusion
  414.5 9.2 %all-gather.2 = bf16[384,1,128]{2,0,1:T(8,128)(2,1)S(1)} all-gather(bf16[192,1,128]{2,0,1:T(8,128)(2,1)S(1)} %pad_maximum_fusion), channel_id=4, replica_groups=mesh['rep'=8,'seq'=2,'tp'=32] {'seq'}, dimensions={0}, use_global_device_ids=true | all-gather | bytes 147456 | tf_op jit(solution)/shard_map/all_gather | solution.py:148
  423.7 0.1 subtract_convert_fusion
  423.9 0.4 fusion.50
  424.3 8.7 %all_gather.15 = bf16[384,128]{1,0:T(8,128)(2,1)S(1)} all-gather(bf16[192,128]{1,0:T(8,128)(2,1)S(1)} %get-tuple-element.19), channel_id=1, replica_groups=mesh['rep'=8,'seq'=2,'tp'=32] {'seq'}, dimensions={0}, use_global_device_ids=true | all-gather | bytes 147456 | tf_op jit(solution)/shard_map/all_gather | solution.py:149
  433.0 0.3 fusion.12
  433.3 0.3 fusion.11
  433.7 0.7 bitcast_select_fusion
  (19 shorter events, 0.2 us)
Async XLA Ops:
  6.5 41.2 %copy-start = (bf16[2,128,2048]{2,1,0:T(8,128)(2,1)S(1)}, bf16[2,128,2048]{2,1,0:T(8,128)(2,1)}, u32[]{:S(2)}) copy-start(bf16[2,128,2048]{2,1,0:T(8,128)(2,1)} %param.9) | copy-start | bytes 3145732
  12.7 34.7 %copy-start.1 = (f32[8192]{0:T(1024)S(1)}, f32[8192]{0:T(1024)}, u32[]{:S(2)}) copy-start(f32[8192]{0:T(1024)} %param.7) | copy-start | bytes 98308
  14.0 18.4 %all-to-all-start = ((bf16[8,192,128]{2,1,0:T(8,128)(2,1)}), bf16[8,192,128]{2,1,0:T(8,128)(2,1)S(1)}, u32[]{:S(2)}, u32[]{:S(2)}) async-start(bf16[8,192,128]{2,1,0:T(8,128)(2,1)} %select_select_fusion), calls=%async_computation | async-start | bytes 786432 | tf_op jit(solution)/shard_map/all_to_all | solution.py:107
  23.1 110.2 %all-gather.6.cloned.1.call-start = ((), (), s32[]{:S(2)}) async-start(), calls=%async_computation.3 | async-start | bytes 3244032 | tf_op jit(solution)/shard_map/all_gather | solution.py:126
  46.6 200.9 %all-gather.8.cloned.1.call-start = ((), (), s32[]{:S(2)}) async-start(), calls=%async_computation.4 | async-start | bytes 6291456 | tf_op jit(solution)/shard_map/all_gather | solution.py:123
  47.3 365.6 %all-reduce.2.cloned.1.call-start = ((), (), s32[]{:S(2)}) async-start(), calls=%async_computation.2 | async-start | bytes 3145728 | tf_op jit(solution)/shard_map/psum | solution.py:140
Sparse Core Ops, SparseCore 0:
  46.7 86.6 all-gather.5
  135.4 111.9 all-gather.7
  250.8 162.0 all-reduce.1
where the time goes:
time: 441 us
  waiting for transfers between devices  365 us (83%)
  blocking collectives  28.5 us (6%)
  between operations  13.4 us (3%)
  starting transfers between devices  9.17 us (2%)
  other arithmetic  9.02 us (2%)
  local copies, waits for them, and re-layouts  8.3 us (2%)
  matrix products  7.34 us (2%)
    psum x1, waiting for transfers between devices, local(): kv_total = lax.psum(kv_partial, 'tp')  161 us
    all_gather x1, waiting for transfers between devices, local(): lax.all_gather(w_query.reshape(1, w_query.shape[0], w_query.shape[1]), 's...  111 us
    all_gather x1, waiting for transfers between devices, local(): feature_piece = lax.all_gather(local_x, 'tp', axis=2, tiled=True)  82.6 us
    all_to_all x1, blocking collectives, local(): lax.all_to_all(assembled.reshape(BUFFER, 1, feature_cols), 'seq', split_a...  10.6 us
    all_gather x1, blocking collectives, local(): key_part = lax.all_gather(keys, 'seq', axis=0, tiled=True)  9.25 us
    all_to_all x1, waiting for transfers between devices, local(): lax.all_to_all(outgoing, 'rep', split_axis=0, concat_axis=0, tiled=True)  9.09 us
    all_to_all x1, starting transfers between devices, local(): lax.all_to_all(outgoing, 'rep', split_axis=0, concat_axis=0, tiled=True)  9.08 us
  transfers between devices with their start and end apart: 4, of which 4 were waited for; matrix products, arithmetic and copies ran while one was open for 2% of the time, Pallas kernels for 0%

commit v1 on v0

--- a/solution.py
+++ b/solution.py
@@ -145,8 +145,11 @@
     values = (inverse_rms[:, None] * head_block[:, HD:]).astype(jnp.bfloat16)
     score_scale = 1.0 / math.sqrt(HD)
     running = jnp.full((local_rows, head_count), MASK_FILL, jnp.float32)
-    key_part = lax.all_gather(keys, "seq", axis=0, tiled=True)
-    value_part = lax.all_gather(values, "seq", axis=0, tiled=True)
+    key_part, value_part = jnp.split(
+        lax.all_gather(jnp.concatenate([keys, values], axis=1), "seq", axis=0, tiled=True),
+        [keys.shape[1]],
+        axis=1,
+    )
     key_count = key_part.shape[0]
     key_pos = jnp.arange(key_count, dtype=jnp.int32)
     key_seg = locate(key_pos, replica, tables)[0]

time: 441 us -> 434 us (0.984)
  blocking collectives: 28.5 us -> 20.9 us
    all_gather x2 -> x1, blocking collectives: 18 us -> 10.3 us  [local(): lax.all_gather(jnp.concatenate([keys, values], axis=1), 'seq', axis=0, ti...]
where the time goes in v1:
time: 434 us; the launch traced here: 433 us
  waiting for transfers between devices  365 us (84%)
  blocking collectives  20.9 us (5%)
  between operations  13.4 us (3%)
  starting transfers between devices  9.17 us (2%)
  other arithmetic  9.05 us (2%)
  local copies, waits for them, and re-layouts  8.3 us (2%)
  matrix products  7.34 us (2%)
    psum x1, waiting for transfers between devices, local(): kv_total = lax.psum(kv_partial, 'tp')  161 us
    all_gather x1, waiting for transfers between devices, local(): lax.all_gather(w_query.reshape(1, w_query.shape[0], w_query.shape[1]), 's...  111 us
    all_gather x1, waiting for transfers between devices, local(): feature_piece = lax.all_gather(local_x, 'tp', axis=2, tiled=True)  82.6 us
    all_to_all x1, blocking collectives, local(): lax.all_to_all(assembled.reshape(BUFFER, 1, feature_cols), 'seq', split_a...  10.6 us
    all_gather x1, blocking collectives, local(): lax.all_gather(jnp.concatenate([keys, values], axis=1), 'seq', axis=0, ti...  10.3 us
    all_to_all x1, waiting for transfers between devices, local(): lax.all_to_all(outgoing, 'rep', split_axis=0, concat_axis=0, tiled=True)  9.09 us
    all_to_all x1, starting transfers between devices, local(): lax.all_to_all(outgoing, 'rep', split_axis=0, concat_axis=0, tiled=True)  9.08 us
  transfers between devices with their start and end apart: 4, of which 4 were waited for; matrix products, arithmetic and copies ran while one was open for 2% of the time, Pallas kernels for 0%

profile of v1, /device:TPU:16, one launch (start us, length us, event | category | flops | bytes accessed | tf_op | source)
XLA Modules:
  0.0 433.3 jit_solution(2389708032764581507)
XLA Ops:
  6.5 0.0 copy-start
  6.5 0.8 copy.25
  7.4 0.1 broadcast_in_dim.98
  7.5 0.8 copy.24
  8.2 0.1 broadcast_in_dim_reshape.2
  8.3 0.1 dynamic_slice.18
  8.4 0.2 select_reduce_fusion.7
  8.6 0.1 dynamic-slice_add_fusion
  8.7 0.1 dynamic_slice.21
  8.8 0.1 iota_compare_fusion.7
  8.8 0.1 select_reduce_fusion.4
  8.9 0.1 reshape.451
  9.0 0.1 fusion.41
  9.1 3.5 gather_fusion
  12.7 0.0 copy-start.1
  12.7 1.3 select_select_fusion
  14.0 9.1 %all-to-all-start = ((bf16[8,192,128]{2,1,0:T(8,128)(2,1)}), bf16[8,192,128]{2,1,0:T(8,128)(2,1)S(1)}, u32[]{:S(2)}, u32[]{:S(2)}) async-start(bf16[8,192,128]{2,1,0:T(8,128)(2,1)} %select_select_fusion), calls=%async_computation | async-start | bytes 786432 | tf_op jit(solution)/shard_map/all_to_all | solution.py:107
  23.1 0.0 all-gather.5.cloned.1.call-start
  23.1 0.1 select_reduce_fusion.1
  23.3 9.1 %all-to-all-done = bf16[8,192,128]{2,1,0:T(8,128)(2,1)S(1)} async-done(((bf16[8,192,128]{2,1,0:T(8,128)(2,1)}), bf16[8,192,128]{2,1,0:T(8,128)(2,1)S(1)}, u32[]{:S(2)}, u32[]{:S(2)}) %all-to-all-start) | async-done | bytes 393248 | tf_op jit(solution)/shard_map/all_to_all | solution.py:107
  32.4 1.4 gather_fusion.1
  33.8 0.2 fusion.35
  34.0 0.5 broadcast.494
  34.5 0.7 reduce.4
  35.2 10.6 %all_to_all.27 = bf16[2,2,12288]{2,1,0:T(2,128)(2,1)S(1)} all-to-all(bf16[2,2,12288]{2,1,0:T(2,128)(2,1)S(1)} %reshape.480), channel_id=1, replica_groups=mesh['rep'=8,'seq'=2,'tp'=32] {'seq'}, dimensions={0} | all-to-all | bytes 196608 | tf_op jit(solution)/shard_map/all_to_all | solution.py:112
  45.8 0.1 reshape.481
  45.9 0.7 copy.29
  46.5 0.0 all-gather.5.cloned.1.call-update
  46.6 0.0 all-gather.7.cloned.1.call-start
  46.6 0.7 all-gather.7.cloned.1.call-update
  47.3 0.0 all-reduce.2.cloned.1.call-start
  47.4 0.0 copy-done.1
  47.5 0.1 select_reduce_fusion.3
  47.6 0.2 fusion.18
  47.8 0.0 copy-done
  47.8 2.5 convolution_bitcast_fusion
  50.2 0.0 all-reduce.2.cloned.1.call-update
  50.3 0.4 multiply_cosine_fusion.1
  50.7 82.6 %all-gather.5.cloned.1.call-done = bf16[192,2,1,4096]{3,0,1,2:T(8,128)(2,1)} async-done(((bf16[192,2,1,128]{3,0,1,2:T(8,128)(2,1)}), bf16[192,2,1,4096]{3,0,1,2:T(8,128)(2,1)}) %all-gather.5.cloned.1.call-update) | async-done | bytes 3145744 | tf_op jit(solution)/shard_map/all_gather | solution.py:126
  133.3 2.6 fusion
  135.9 111.5 %all-gather.7.cloned.1.call-done = bf16[8192,256]{1,0:T(8,128)(2,1)} async-done(((bf16[4096,256]{1,0:T(8,128)(2,1)}), bf16[8192,256]{1,0:T(8,128)(2,1)}) %all-gather.7.cloned.1.call-update) | async-done | bytes 4194320 | tf_op jit(solution)/shard_map/all_gather | solution.py:123
  247.4 4.1 fusion.7
  251.6 0.1 bitcast_multiply_fusion
  251.7 161.3 %all-reduce.2.cloned.1.call-done = f32[192,2048]{1,0:T(8,128)} async-done(((f32[192,2048]{1,0:T(8,128)}), f32[192,2048]{1,0:T(8,128)}) %all-reduce.2.cloned.1.call-update) | async-done | bytes 1572880 | tf_op jit(solution)/shard_map/psum | solution.py:140
  412.9 1.0 fusion.31
  413.9 0.5 fusion.26
  414.4 0.1 maximum_bitcast_fusion
  414.5 10.3 %all_gather.11 = bf16[384,256]{1,0:T(8,128)(2,1)S(1)} all-gather(bf16[192,256]{1,0:T(8,128)(2,1)S(1)} %pad_maximum_fusion), channel_id=1, replica_groups=mesh['rep'=8,'seq'=2,'tp'=32] {'seq'}, dimensions={0}, use_global_device_ids=true | all-gather | bytes 294912 | tf_op jit(solution)/shard_map/all_gather | solution.py:149
  424.8 0.1 subtract_convert_fusion
  425.0 0.4 fusion.48
  425.4 0.3 fusion.12
  425.7 0.3 fusion.11
  426.0 0.7 bitcast_select_fusion
  (20 shorter events, 0.2 us)
Async XLA Ops:
  6.5 41.2 %copy-start = (bf16[2,128,2048]{2,1,0:T(8,128)(2,1)S(1)}, bf16[2,128,2048]{2,1,0:T(8,128)(2,1)}, u32[]{:S(2)}) copy-start(bf16[2,128,2048]{2,1,0:T(8,128)(2,1)} %param.9) | copy-start | bytes 3145732
  12.7 34.7 %copy-start.1 = (f32[8192]{0:T(1024)S(1)}, f32[8192]{0:T(1024)}, u32[]{:S(2)}) copy-start(f32[8192]{0:T(1024)} %param.7) | copy-start | bytes 98308
  14.0 18.4 %all-to-all-start = ((bf16[8,192,128]{2,1,0:T(8,128)(2,1)}), bf16[8,192,128]{2,1,0:T(8,128)(2,1)S(1)}, u32[]{:S(2)}, u32[]{:S(2)}) async-start(bf16[8,192,128]{2,1,0:T(8,128)(2,1)} %select_select_fusion), calls=%async_computation | async-start | bytes 786432 | tf_op jit(solution)/shard_map/all_to_all | solution.py:107
  23.1 110.2 %all-gather.5.cloned.1.call-start = ((), (), s32[]{:S(2)}) async-start(), calls=%async_computation.3 | async-start | bytes 3244032 | tf_op jit(solution)/shard_map/all_gather | solution.py:126
  46.6 200.9 %all-gather.7.cloned.1.call-start = ((), (), s32[]{:S(2)}) async-start(), calls=%async_computation.4 | async-start | bytes 6291456 | tf_op jit(solution)/shard_map/all_gather | solution.py:123
  47.3 365.6 %all-reduce.2.cloned.1.call-start = ((), (), s32[]{:S(2)}) async-start(), calls=%async_computation.2 | async-start | bytes 3145728 | tf_op jit(solution)/shard_map/psum | solution.py:140
Sparse Core Ops, SparseCore 0:
  46.7 86.6 all-gather.4
  135.4 111.9 all-gather.6
  250.8 162.0 all-reduce.1
